TPU v7x, 128 devices: a whole 4x4x4 slice. The times are simulated.
128 devices in a mesh: gx: 32 (over x, y_lo, z), gy: 4 (over y_hi, core).
Axes of the slice: x: 4, y: 4 (y_hi: 2, y_lo: 2; y = y_hi * 2 + y_lo), z: 4, core: 2. Of those that a mesh axis runs over, the one named last changes fastest.
Arguments:
- field_in: bfloat16 [20, 128, 128, 1024], P(None, 'gx', 'gy'), may hold values from -6 to 6
- cotangent: bfloat16 [20, 128, 128, 1024], P(None, 'gx', 'gy'), may hold values from -6 to 6
- spec_weight: float32 [2, 192, 20, 20, 24, 24], P(None, 'gx', None, None, 'gy'), may hold values from -6 to 6
Outputs:
- grad_field: bfloat16 [20, 128, 128, 1024], P(None, 'gx', 'gy')
- grad_weight: float32 [2, 192, 20, 20, 24, 24], P(None, 'gx', None, None, 'gy')
All inputs are finite; a program needn't handle non-finite values.
Results may differ from a plain program's by a relative error of at most 0.001.
Values sent between devices are 32-bit elements; how exact they have to be, the bound alone decides.
No kernel may reach another device: no remote copies, remote signals or barrier semaphores. Data moves between devices by JAX's collectives and lax.ppermute only.
A program may use at most 512 MiB of HBM per device.

v0:
```python
import math

import jax
import jax.numpy as jnp
from jax import lax
from jax.sharding import PartitionSpec as P

MX = 12
MY = 12
MZ = 12
MT = 8
Z = 64
T_SIZE = 16
KX = 24
KY = 24
M = 192


exact_precision = lax.Precision.HIGHEST
split_precision = lax.Precision.HIGH
lead_contract = (((0,), (0,)), ((), ()))
tail_contract = (((1,), (1,)), ((), ()))


def signed_freqs(count, half_count):
    ladder = lax.iota(jnp.int32, count)
    return jnp.where(ladder < half_count, ladder, ladder - 2 * half_count)


def pair_table(frequencies, length):
    places = lax.iota(jnp.int32, length)
    residue = jnp.remainder(frequencies[:, None] * places[None, :], length)
    phases = residue.astype(jnp.float32) * (2.0 * math.pi / length)
    cosine = jnp.cos(phases) / math.sqrt(length)
    sines = jnp.sin(phases) / math.sqrt(length)
    return jnp.stack([jnp.stack([cosine, sines]), jnp.stack([-sines, cosine])])


def depth_rows_table():
    cell_ids = lax.iota(jnp.int32, Z * T_SIZE)
    depth_index = cell_ids // T_SIZE
    time_index = cell_ids % T_SIZE
    mode_ids = lax.iota(jnp.int32, M)
    depth_freq = mode_ids // MT
    depth_freq = jnp.where(depth_freq < MZ, depth_freq, depth_freq - 2 * MZ)
    time_freq = mode_ids % MT
    residue = jnp.remainder(
        depth_freq[:, None] * depth_index[None, :] * T_SIZE
        + time_freq[:, None] * time_index[None, :] * Z,
        Z * T_SIZE,
    )
    phases = residue.astype(jnp.float32) * (2.0 * math.pi / (Z * T_SIZE))
    factor = 1.0 / math.sqrt(Z * T_SIZE)
    return jnp.stack([jnp.cos(phases) * factor, -jnp.sin(phases) * factor])


def split_table(table):
    leading = table.astype(jnp.bfloat16)
    residual_part = (table - lax.optimization_barrier(leading).astype(jnp.float32)).astype(
        jnp.bfloat16
    )
    return (leading, residual_part)


def per_device(field_in, cotangent, spec_weight):
    channels, x_local, y_local, depth_time = field_in.shape
    x_groups = lax.axis_size("gx")
    x_count = x_local * x_groups
    y_count = y_local * lax.axis_size("gy")
    mode_local = M // x_groups
    x_table = pair_table(signed_freqs(KX, MX), x_count)
    x_blocks = x_table.reshape(2, 2, KX, x_groups, x_local)
    y_table = pair_table(signed_freqs(KY, MY), y_count)
    depth_modes = depth_rows_table()
    depth_flat = depth_modes.reshape(2 * M, depth_time)
    chunk_rows = depth_modes.reshape(2, x_groups, mode_local, depth_time).transpose(1, 0, 2, 3)
    depth_lead, depth_tail = split_table(chunk_rows.reshape(2 * M, depth_time))
    y_parts = lax.axis_size("gy")
    kx_local = KX // y_parts
    y_split = y_table.reshape(2, 2, KY, y_parts, y_local)

    def depth_forward(flat_rows):
        first = lax.dot_general(
            depth_lead, flat_rows, tail_contract, preferred_element_type=jnp.float32
        )
        return first + lax.dot_general(
            depth_tail, flat_rows, tail_contract, preferred_element_type=jnp.float32
        )

    def field_modes(field):
        slabs = [
            depth_forward(field[:, plane].reshape(channels * y_local, depth_time)).reshape(
                x_groups, 2 * mode_local, channels * y_local
            )
            for plane in range(x_local)
        ]
        spectra = jnp.stack(slabs, axis=1).reshape(
            x_groups, x_local, 2, mode_local, channels * y_local
        )
        section = lax.all_to_all(spectra, "gx", split_axis=0, concat_axis=0, tiled=True)
        summed_x = jnp.einsum("pqkbx,bxqjn->pkjn", x_blocks, section, precision=split_precision)
        summed_x = summed_x.reshape(2, y_parts, kx_local, mode_local, channels * y_local)
        summed_x = summed_x.transpose(1, 0, 2, 3, 4)
        gathered = lax.all_to_all(summed_x, "gy", split_axis=0, concat_axis=0, tiled=True)
        gathered = gathered.reshape(gathered.shape[:4] + (channels, y_local))
        return jnp.einsum("pqksy,sqajcy->pjcak", y_split, gathered, precision=split_precision)

    at_modes = jnp.stack([field_modes(field_in), field_modes(cotangent)])
    mode_ids = lax.axis_index("gx") * mode_local + lax.iota(jnp.int32, mode_local)
    doubling = jnp.where(mode_ids % MT == 0, 1.0, 2.0).astype(jnp.float32)[:, None, None, None]
    field_real = at_modes[0, 0]
    field_imag = at_modes[0, 1]
    dual_real = at_modes[1, 0] * doubling
    dual_imag = at_modes[1, 1] * doubling
    grad_real = (
        field_real[:, :, None] * dual_real[:, None] + field_imag[:, :, None] * dual_imag[:, None]
    )
    grad_imag = (
        field_real[:, :, None] * dual_imag[:, None] - field_imag[:, :, None] * dual_real[:, None]
    )
    grad_weight = jnp.stack([grad_real, grad_imag])
    back_real = jnp.sum(
        spec_weight[0] * dual_real[:, None] + spec_weight[1] * dual_imag[:, None], axis=2
    )
    back_imag = jnp.sum(
        spec_weight[0] * dual_imag[:, None] - spec_weight[1] * dual_real[:, None], axis=2
    )
    backward = jnp.stack([back_real, back_imag])
    y_parts = lax.axis_size("gy")
    y_chunks = y_table.reshape(2, 2, KY, y_parts, y_local)
    spread = jnp.einsum("qpkdy,qjcak->dpajcy", y_chunks, backward, precision=split_precision)
    spread = spread.reshape(spread.shape[:4] + (channels * y_local,))
    y_done = lax.all_to_all(spread, "gy", split_axis=0, concat_axis=0, tiled=True)
    x_inverse = x_table.reshape(2, 2, y_parts, KX // y_parts, x_groups, x_local)
    x_spread = jnp.einsum("pqsabx,spajn->bxqjn", x_inverse, y_done, precision=split_precision)
    section = lax.all_to_all(x_spread, "gx", split_axis=0, concat_axis=0, tiled=True)
    depth_parts = depth_flat.reshape(2, x_groups, mode_local, depth_time)
    summed = jnp.einsum("sxqjn,qsjz->xnz", section, depth_parts, precision=split_precision)
    summed = lax.optimization_barrier(summed.astype(jnp.bfloat16))
    grad_field = summed.reshape(x_local, channels, y_local, depth_time).transpose(1, 0, 2, 3)
    return (grad_field, grad_weight)


def solution(mesh):
    in_specs = (
        P(None, "gx", "gy", None),
        P(None, "gx", "gy", None),
        P(None, "gx", None, None, "gy", None),
    )
    out_specs = (P(None, "gx", "gy", None), P(None, "gx", None, None, "gy", None))
    return jax.shard_map(
        per_device, mesh=mesh, in_specs=in_specs, out_specs=out_specs, check_vma=False
    )
```

profile of v0, /device:TPU:37, one launch (start us, length us, event | category | flops | bytes accessed | tf_op | source)
XLA Modules:
  0.0 312.3 jit_solution(2540907579753461590)
XLA Ops:
  0.7 3.3 %cosine_multiply_fusion = (f32[1,32,6,1024]{3,1,0,2:T(8,128)S(1)}, f32[1,32,6,1024]{3,1,0,2:T(8,128)S(1)}) fusion(s32[1024]{0:T(1024)S(1)} %get-tuple-element.33, s32[32,6]{0,1:T(8,128)S(1)} %get-tuple-element.32, s32[1024]{0:T(1024)S(1)} %get-tuple-element.34, s32[32,6]{0,1:T(8,128)S(1)} %get-tuple-element.31), kind=kLoop, calls=%fused_computation.56 | loop fusion | flops 4128768 | bytes 1582592 | tf_op jit(solution)/shard_map/mul | solution.py:54
  10.5 5.1 %fusion.75 = (bf16[20,1,32,1024]{3,2,1,0:T(8,128)(2,1)S(1)}, bf16[20,1,32,1024]{3,2,1,0:T(8,128)(2,1)}, bf16[20,1,32,1024]{3,2,1,0:T(8,128)(2,1)S(1)}, bf16[20,1,32,1024]{3,2,1,0:T(8,128)(2,1)}) fusion(bf16[20,4,32,1024]{3,2,1,0:T(8,128)(2,1)} %param.4), kind=kLoop, calls=%fused_computation.145 | loop fusion | bytes 10485760 | tf_op jit(solution)/shard_map/slice | solution.py:92
  19.6 2.5 fusion.77
  26.3 2.5 fusion.78
  41.3 4.5 %copy.85 = f32[32,4,2,6,640]{4,1,2,3,0:T(4,128)} copy(f32[32,4,2,6,640]{4,3,2,0,1:T(8,128)S(1)} %pad_maximum_fusion.1) | data formatting | bytes 7864320 | tf_op jit(solution)/shard_map/stack | solution.py:97
  45.8 9.2 %all-to-all-start = ((f32[32,4,2,6,640]{4,1,2,3,0:T(4,128)}), f32[32,4,2,6,640]{4,1,2,3,0:T(4,128)}, u32[]{:S(2)}, u32[]{:S(2)}) async-start(f32[32,4,2,6,640]{4,1,2,3,0:T(4,128)} %copy.85), calls=%async_computation | async-start | bytes 7864320 | tf_op jit(solution)/shard_map/all_to_all | solution.py:100
  55.0 4.9 %fusion.74 = (bf16[20,1,32,1024]{3,2,1,0:T(8,128)(2,1)S(1)}, bf16[20,1,32,1024]{3,2,1,0:T(8,128)(2,1)}, bf16[20,1,32,1024]{3,2,1,0:T(8,128)(2,1)S(1)}, bf16[20,1,32,1024]{3,2,1,0:T(8,128)(2,1)}) fusion(bf16[20,4,32,1024]{3,2,1,0:T(8,128)(2,1)} %param.3), kind=kLoop, calls=%fused_computation.144 | loop fusion | bytes 10485760 | tf_op jit(solution)/shard_map/slice | solution.py:92
  63.9 2.5 fusion.81
  85.6 4.4 %copy.101 = f32[32,4,2,6,640]{4,1,2,3,0:T(4,128)} copy(f32[32,4,2,6,640]{4,3,2,0,1:T(8,128)S(1)} %pad_maximum_fusion.2) | data formatting | bytes 7864320 | tf_op jit(solution)/shard_map/stack | solution.py:97
  90.0 16.6 %all-to-all-done = f32[32,4,2,6,640]{4,1,2,3,0:T(4,128)} async-done(((f32[32,4,2,6,640]{4,1,2,3,0:T(4,128)}), f32[32,4,2,6,640]{4,1,2,3,0:T(4,128)}, u32[]{:S(2)}, u32[]{:S(2)}) %all-to-all-start) | async-done | bytes 3932192 | tf_op jit(solution)/shard_map/all_to_all | solution.py:100
  106.6 5.7 %all-to-all-start.4 = ((f32[32,4,2,6,640]{4,1,2,3,0:T(4,128)}), f32[32,4,2,6,640]{4,1,2,3,0:T(4,128)}, u32[]{:S(2)}, u32[]{:S(2)}) async-start(f32[32,4,2,6,640]{4,1,2,3,0:T(4,128)} %copy.101), calls=%async_computation.4 | async-start | bytes 7864320 | tf_op jit(solution)/shard_map/all_to_all | solution.py:100
  114.1 15.8 %fusion.73 = (f32[1,6,20,20,6,24]{5,0,4,3,2,1:T(1,128)}, f32[1,6,20,20,6,24]{5,0,4,3,2,1:T(1,128)}) fusion(f32[2,6,20,20,6,24]{5,0,4,3,2,1:T(2,128)} %param.5), kind=kLoop, calls=%fused_computation.143 | loop fusion | bytes 5529600 | tf_op jit(solution)/shard_map/slice | solution.py:123
  129.9 6.4 %fusion.21 = f32[4,2,6,6,640]{4,2,3,0,1:T(8,128)S(1)} fusion(f32[32,4,2,6,640,1,1]{4,1,2,3,0,6,5:T(4,128)} %bitcast.9, f32[2,4,6,32,2,4,1]{3,5,4,2,1,0,6:T(4,128)S(1)} %bitcast.195), kind=kOutput, calls=%fused_computation.32 | convolution fusion | flops 283115520 | bytes 4718592 | tf_op jit(solution)/shard_map/pqkbx,bxqjn->pkjn/dot_general | solution.py:101
  137.7 28.1 %all-to-all-done.4 = f32[32,4,2,6,640]{4,1,2,3,0:T(4,128)} async-done(((f32[32,4,2,6,640]{4,1,2,3,0:T(4,128)}), f32[32,4,2,6,640]{4,1,2,3,0:T(4,128)}, u32[]{:S(2)}, u32[]{:S(2)}) %all-to-all-start.4) | async-done | bytes 3932192 | tf_op jit(solution)/shard_map/all_to_all | solution.py:100
  165.8 4.7 %all-to-all-start.1 = ((f32[4,2,6,6,640]{4,1,3,2,0:T(2,128)}), f32[4,2,6,6,640]{4,1,3,2,0:T(2,128)}, u32[]{:S(2)}, u32[]{:S(2)}) async-start(f32[4,2,6,6,640]{4,1,3,2,0:T(2,128)} %copy.88), calls=%async_computation.1 | async-start | bytes 1474560 | tf_op jit(solution)/shard_map/all_to_all | solution.py:104
  170.9 6.4 %fusion.24 = f32[4,2,6,6,640]{4,2,3,0,1:T(8,128)S(1)} fusion(f32[32,4,2,6,640,1,1]{4,1,2,3,0,6,5:T(4,128)} %bitcast.48, f32[2,4,6,32,2,4,1]{3,5,4,2,1,0,6:T(4,128)S(1)} %bitcast.196), kind=kOutput, calls=%fused_computation.33 | convolution fusion | flops 283115520 | bytes 4718592 | tf_op jit(solution)/shard_map/pqkbx,bxqjn->pkjn/dot_general | solution.py:101
  178.7 3.6 %all-to-all-done.1 = f32[4,2,6,6,640]{4,1,3,2,0:T(2,128)} async-done(((f32[4,2,6,6,640]{4,1,3,2,0:T(2,128)}), f32[4,2,6,6,640]{4,1,3,2,0:T(2,128)}, u32[]{:S(2)}, u32[]{:S(2)}) %all-to-all-start.1) | async-done | bytes 737312 | tf_op jit(solution)/shard_map/all_to_all | solution.py:104
  182.3 5.6 %all-to-all-start.5 = ((f32[4,2,6,6,640]{4,1,3,2,0:T(2,128)}), f32[4,2,6,6,640]{4,1,3,2,0:T(2,128)}, u32[]{:S(2)}, u32[]{:S(2)}) async-start(f32[4,2,6,6,640]{4,1,3,2,0:T(2,128)} %copy.104), calls=%async_computation.5 | async-start | bytes 1474560 | tf_op jit(solution)/shard_map/all_to_all | solution.py:104
  187.9 4.0 %reshape.565 = f32[4,2,6,6,20,32,1]{5,4,1,3,2,0,6:T(8,128)} reshape(f32[4,2,6,6,640]{4,1,3,2,0:T(2,128)} %all-to-all-done.1) | data formatting | bytes 1474560 | tf_op jit(solution)/shard_map/reshape | solution.py:105
  191.9 3.7 %fusion.16 = f32[6,6,20,2,24,1,1]{4,2,5,3,1,0,6:T(8,128)S(1)} fusion(f32[4,2,6,6,20,32,1]{5,4,1,3,2,0,6:T(8,128)} %reshape.565, f32[1,1,24,4,32]{4,2,1,0,3:T(8,128)S(1)} %get-tuple-element.27, f32[1,1,24,4,32]{4,2,1,0,3:T(8,128)S(1)} %get-tuple-element.26, f32[1,1,24,4,32]{4,2,1,0,3:T(8,128)S(1)} %get-tuple-element.25), kind=kOutput, calls=%fused_computation.25 | convolution fusion | flops 53121024 | bytes 912384 | tf_op jit(solution)/shard_map/pqksy,sqajcy->pjcak/dot_general | solution.py:106
  195.8 9.3 %fusion.3 = (f32[6,20,6,24]{3,2,1,0:T(8,128)S(1)}, f32[6,20,6,24]{3,2,1,0:T(8,128)S(1)}) fusion(f32[1,6,20,20,6,24]{5,0,4,3,2,1:T(1,128)} %get-tuple-element.5, f32[1,6,20,20,6,24]{5,0,4,3,2,1:T(1,128)S(1)} %bitcast.174, f32[6,20,6,24]{3,1,0,2:T(8,128)S(1)} %get-tuple-element.16, f32[6,20,6,24]{3,1,0,2:T(8,128)S(1)} %get-tuple-element.17), kind=kLoop, calls=%fused_computation.6 | loop fusion | flops 2730240 | bytes 3041280 | tf_op jit(solution)/shard_map/reduce_sum | solution.py:122
  212.9 5.2 %all-to-all-start.2 = ((f32[4,2,6,6,640]{4,1,3,2,0:T(2,128)}), f32[4,2,6,6,640]{4,1,3,2,0:T(2,128)}, u32[]{:S(2)}, u32[]{:S(2)}) async-start(f32[4,2,6,6,640]{4,1,3,2,0:T(2,128)} %copy.133), calls=%async_computation.2 | async-start | bytes 1474560 | tf_op jit(solution)/shard_map/all_to_all | solution.py:133
  218.1 2.9 reshape.579
  223.8 6.0 %all-to-all-done.2 = f32[4,2,6,6,640]{4,1,3,2,0:T(2,128)} async-done(((f32[4,2,6,6,640]{4,1,3,2,0:T(2,128)}), f32[4,2,6,6,640]{4,1,3,2,0:T(2,128)}, u32[]{:S(2)}, u32[]{:S(2)}) %all-to-all-start.2) | async-done | bytes 737312 | tf_op jit(solution)/shard_map/all_to_all | solution.py:133
  229.8 2.9 convolution_bitcast_fusion
  232.7 5.0 %copy.98 = f32[32,4,2,6,640]{4,2,3,1,0:T(2,128)} copy(f32[32,4,2,6,640]{4,0,2,3,1:T(8,128)S(1)} %convolution_bitcast_fusion) | data formatting | bytes 7864320 | tf_op jit(solution)/shard_map/pqsabx,spajn->bxqjn/transpose | solution.py:135
  237.7 5.8 %all-to-all-start.3 = ((f32[32,4,2,6,640]{4,2,3,1,0:T(2,128)}), f32[32,4,2,6,640]{4,2,3,1,0:T(2,128)}, u32[]{:S(2)}, u32[]{:S(2)}) async-start(f32[32,4,2,6,640]{4,2,3,1,0:T(2,128)} %copy.98), calls=%async_computation.3 | async-start | bytes 7864320 | tf_op jit(solution)/shard_map/all_to_all | solution.py:136
  243.5 12.6 %multiply_add_fusion = (f32[1,6,20,20,6,24]{5,0,4,3,2,1:T(1,128)S(1)}, f32[1,6,20,20,6,24]{5,0,4,3,2,1:T(1,128)S(1)}) fusion(f32[6,20,6,24]{3,2,1,0:T(8,128)S(1)} %copy-done.11, f32[6,20,6,24]{3,2,1,0:T(8,128)S(1)} %copy.107, f32[6,20,6,24]{3,2,1,0:T(8,128)S(1)} %copy-done.10, f32[6,20,6,24]{3,2,1,0:T(8,128)S(1)} %copy.105), kind=kLoop, calls=%fused_computation.13 | loop fusion | flops 2073600 | bytes 3041280 | tf_op jit(solution)/shard_map/add | solution.py:116
  256.1 17.3 %pad_maximum_fusion = f32[2,6,20,20,6,24]{5,0,4,3,2,1:T(2,128)} fusion(f32[1,6,20,20,6,24]{5,0,4,3,2,1:T(1,128)S(1)} %get-tuple-element.15, f32[1,6,20,20,6,24]{5,0,4,3,2,1:T(1,128)S(1)} %get-tuple-element.14), kind=kLoop, calls=%fused_computation | loop fusion | flops 691200 | bytes 5529600 | tf_op jit(solution)/shard_map/stack | solution.py:121
  273.5 24.8 %all-to-all-done.3 = f32[32,4,2,6,640]{4,2,3,1,0:T(2,128)} async-done(((f32[32,4,2,6,640]{4,2,3,1,0:T(2,128)}), f32[32,4,2,6,640]{4,2,3,1,0:T(2,128)}, u32[]{:S(2)}, u32[]{:S(2)}) %all-to-all-start.3) | async-done | bytes 3932192 | tf_op jit(solution)/shard_map/all_to_all | solution.py:136
  298.3 10.8 %bitcast_convert_fusion = bf16[4,640,1024]{2,1,0:T(8,128)(2,1)S(1)} fusion(f32[32,4,2,6,640]{4,2,3,1,0:T(2,128)} %all-to-all-done.3, f32[1,32,6,1024]{3,1,0,2:T(8,128)S(1)} %copy-done.3, f32[1,32,6,1024]{3,1,0,2:T(8,128)S(1)} %copy-done.1), kind=kOutput, calls=%fused_computation.1 | convolution fusion | flops 6042812416 | bytes 10747904 | tf_op jit(solution)/shard_map/sxqjn,qsjz->xnz/dot_general | solution.py:138
  309.1 3.0 copy.197
  (107 shorter events, 66.0 us)
Async XLA Ops:
  4.0 0.9 copy-start
  4.0 1.1 copy-start.2
  10.5 5.1 %copy-start.19 = (bf16[384,1024]{1,0:T(8,128)(2,1)}, bf16[384,1024]{1,0:T(8,128)(2,1)S(1)}, u32[]{:S(2)}) copy-start(bf16[384,1024]{1,0:T(8,128)(2,1)S(1)} %convert_element_type.114) | copy-start | bytes 2359300
  19.6 2.5 copy-start.8
  26.3 2.5 copy-start.5
  36.7 2.5 copy-start.6
  45.8 60.8 %all-to-all-start = ((f32[32,4,2,6,640]{4,1,2,3,0:T(4,128)}), f32[32,4,2,6,640]{4,1,2,3,0:T(4,128)}, u32[]{:S(2)}, u32[]{:S(2)}) async-start(f32[32,4,2,6,640]{4,1,2,3,0:T(4,128)} %copy.85), calls=%async_computation | async-start | bytes 7864320 | tf_op jit(solution)/shard_map/all_to_all | solution.py:100
  55.0 4.9 %copy-start.20 = (bf16[384,1024]{1,0:T(8,128)(2,1)S(1)}, bf16[384,1024]{1,0:T(8,128)(2,1)}, u32[]{:S(2)}) copy-start(bf16[384,1024]{1,0:T(8,128)(2,1)} %copy-done.19) | copy-start | bytes 2359300
  63.8 2.5 copy-start.9
  70.5 2.5 copy-start.7
  80.9 2.5 copy-start.4
  106.6 59.2 %all-to-all-start.4 = ((f32[32,4,2,6,640]{4,1,2,3,0:T(4,128)}), f32[32,4,2,6,640]{4,1,2,3,0:T(4,128)}, u32[]{:S(2)}, u32[]{:S(2)}) async-start(f32[32,4,2,6,640]{4,1,2,3,0:T(4,128)} %copy.101), calls=%async_computation.4 | async-start | bytes 7864320 | tf_op jit(solution)/shard_map/all_to_all | solution.py:100
  165.8 16.4 %all-to-all-start.1 = ((f32[4,2,6,6,640]{4,1,3,2,0:T(2,128)}), f32[4,2,6,6,640]{4,1,3,2,0:T(2,128)}, u32[]{:S(2)}, u32[]{:S(2)}) async-start(f32[4,2,6,6,640]{4,1,3,2,0:T(2,128)} %copy.88), calls=%async_computation.1 | async-start | bytes 1474560 | tf_op jit(solution)/shard_map/all_to_all | solution.py:104
  170.8 21.0 %copy-start.13 = (f32[1,1,24,4,32]{4,2,1,0,3:T(8,128)}, f32[1,1,24,4,32]{4,2,1,0,3:T(8,128)S(1)}, u32[]{:S(2)}) copy-start(f32[1,1,24,4,32]{4,2,1,0,3:T(8,128)S(1)} %get-tuple-element.25) | copy-start | bytes 36868
  170.9 21.0 %copy-start.15 = (f32[1,1,24,4,32]{4,2,1,0,3:T(8,128)}, f32[1,1,24,4,32]{4,2,1,0,3:T(8,128)S(1)}, u32[]{:S(2)}) copy-start(f32[1,1,24,4,32]{4,2,1,0,3:T(8,128)S(1)} %get-tuple-element.26) | copy-start | bytes 36868
  170.9 21.0 %copy-start.17 = (f32[1,1,24,4,32]{4,2,1,0,3:T(8,128)}, f32[1,1,24,4,32]{4,2,1,0,3:T(8,128)S(1)}, u32[]{:S(2)}) copy-start(f32[1,1,24,4,32]{4,2,1,0,3:T(8,128)S(1)} %get-tuple-element.27) | copy-start | bytes 36868
  182.3 13.5 %slice-start = ((s8[7372800]{0:T(1024)(128)(4,1)}), s8[3178496]{0:T(1024)(128)(4,1)S(1)}, s32[]{:S(2)}) async-start(s8[7372800]{0:T(1024)(128)(4,1)} %bitcast.173), calls=%async_computation.6 | async-start | bytes 6356992
  182.3 30.6 %all-to-all-start.5 = ((f32[4,2,6,6,640]{4,1,3,2,0:T(2,128)}), f32[4,2,6,6,640]{4,1,3,2,0:T(2,128)}, u32[]{:S(2)}, u32[]{:S(2)}) async-start(f32[4,2,6,6,640]{4,1,3,2,0:T(2,128)} %copy.104), calls=%async_computation.5 | async-start | bytes 1474560 | tf_op jit(solution)/shard_map/all_to_all | solution.py:104
  191.9 3.9 %slice-start.1 = ((s8[7372800]{0:T(1024)(128)(4,1)}), s8[4194304]{0:T(1024)(128)(4,1)S(1)}, s32[]{:S(2)}) async-start(s8[7372800]{0:T(1024)(128)(4,1)} %bitcast.173), calls=%async_computation.7 | async-start | bytes 8388608
  206.1 1.1 copy-start.14
  206.1 1.1 copy-start.16
  206.1 1.1 copy-start.18
  212.9 16.9 %all-to-all-start.2 = ((f32[4,2,6,6,640]{4,1,3,2,0:T(2,128)}), f32[4,2,6,6,640]{4,1,3,2,0:T(2,128)}, u32[]{:S(2)}, u32[]{:S(2)}) async-start(f32[4,2,6,6,640]{4,1,3,2,0:T(2,128)} %copy.133), calls=%async_computation.2 | async-start | bytes 1474560 | tf_op jit(solution)/shard_map/all_to_all | solution.py:133
  223.5 6.3 %copy-start.12 = (f32[2,2,4,6,32,4,1]{4,5,3,2,1,0,6:T(4,128)S(1)}, f32[2,2,4,6,32,4,1]{4,5,3,2,1,0,6:T(4,128)}, u32[]{:S(2)}) copy-start(f32[2,2,4,6,32,4,1]{4,5,3,2,1,0,6:T(4,128)} %maximum_bitcast_fusion.2) | copy-start | bytes 147460
  237.7 5.9 %copy-start.10 = (f32[6,20,6,24]{3,2,1,0:T(8,128)S(1)}, f32[6,20,6,24]{3,2,1,0:T(8,128)}, u32[]{:S(2)}) copy-start(f32[6,20,6,24]{3,2,1,0:T(8,128)} %copy.106) | copy-start | bytes 207364
  237.7 5.9 %copy-start.11 = (f32[6,20,6,24]{3,2,1,0:T(8,128)S(1)}, f32[6,20,6,24]{3,2,1,0:T(8,128)}, u32[]{:S(2)}) copy-start(f32[6,20,6,24]{3,2,1,0:T(8,128)} %copy.108) | copy-start | bytes 207364
  237.7 60.6 %all-to-all-start.3 = ((f32[32,4,2,6,640]{4,2,3,1,0:T(2,128)}), f32[32,4,2,6,640]{4,2,3,1,0:T(2,128)}, u32[]{:S(2)}, u32[]{:S(2)}) async-start(f32[32,4,2,6,640]{4,2,3,1,0:T(2,128)} %copy.98), calls=%async_computation.3 | async-start | bytes 7864320 | tf_op jit(solution)/shard_map/all_to_all | solution.py:136
  256.1 42.2 %copy-start.1 = (f32[1,32,6,1024]{3,1,0,2:T(8,128)S(1)}, f32[1,32,6,1024]{3,1,0,2:T(8,128)}, u32[]{:S(2)}) copy-start(f32[1,32,6,1024]{3,1,0,2:T(8,128)} %copy-done) | copy-start | bytes 2359300
  256.1 42.2 %copy-start.3 = (f32[1,32,6,1024]{3,1,0,2:T(8,128)S(1)}, f32[1,32,6,1024]{3,1,0,2:T(8,128)}, u32[]{:S(2)}) copy-start(f32[1,32,6,1024]{3,1,0,2:T(8,128)} %copy-done.2) | copy-start | bytes 2359300
where the time goes:
time: 317 us; the launch traced here: 312 us
  local copies, waits for them, and re-layouts  82 us (26%)
  waiting for transfers between devices  79.1 us (25%)
  matrix products  63.9 us (20%)
  other arithmetic  49.7 us (16%)
  starting transfers between devices  36.3 us (11%)
    all_to_all x2, waiting for transfers between devices, field_modes(): lax.all_to_all(spectra, 'gx', split_axis=0, concat_axis=0, tiled=True)  44.7 us
    another operation x10, local copies, waits for them, and re-layouts, field_modes(): jnp.stack(slabs, axis=1)  26 us
    all_to_all x1, waiting for transfers between devices, per_device(): lax.all_to_all(x_spread, 'gx', split_axis=0, concat_axis=0, tiled=True)  24.8 us
    another operation x1, other arithmetic, per_device(): grad_weight = jnp.stack([grad_real, grad_imag])  17.3 us
    slice x1, local copies, waits for them, and re-layouts, per_device(): spec_weight[0] * dual_real[:, None] + spec_weight[1] * dual_imag[:, None]  15.8 us
    dot_general x8, matrix products, depth_forward(): lax.dot_general(depth_lead, flat_rows, tail_contract, preferred_element_t...  15.4 us
    all_to_all x2, starting transfers between devices, field_modes(): lax.all_to_all(spectra, 'gx', split_axis=0, concat_axis=0, tiled=True)  14.9 us
    dot_general x8, matrix products, depth_forward(): lax.dot_general(depth_tail, flat_rows, tail_contract, preferred_element_t...  14.3 us
  transfers between devices with their start and end apart: 6, of which 5 were waited for; matrix products, arithmetic and copies ran while one was open for 41% of the time, Pallas kernels for 0%

commit v1 on v0

--- a/solution.py
+++ b/solution.py
@@ -105,26 +105,28 @@
         gathered = gathered.reshape(gathered.shape[:4] + (channels, y_local))
         return jnp.einsum("pqksy,sqajcy->pjcak", y_split, gathered, precision=split_precision)
 
-    at_modes = jnp.stack([field_modes(field_in), field_modes(cotangent)])
+    dual_modes = field_modes(cotangent)
+    field_spectrum = field_modes(field_in)
     mode_ids = lax.axis_index("gx") * mode_local + lax.iota(jnp.int32, mode_local)
     doubling = jnp.where(mode_ids % MT == 0, 1.0, 2.0).astype(jnp.float32)[:, None, None, None]
-    field_real = at_modes[0, 0]
-    field_imag = at_modes[0, 1]
-    dual_real = at_modes[1, 0] * doubling
-    dual_imag = at_modes[1, 1] * doubling
-    grad_real = (
-        field_real[:, :, None] * dual_real[:, None] + field_imag[:, :, None] * dual_imag[:, None]
-    )
-    grad_imag = (
-        field_real[:, :, None] * dual_imag[:, None] - field_imag[:, :, None] * dual_real[:, None]
-    )
-    grad_weight = jnp.stack([grad_real, grad_imag])
-    back_real = jnp.sum(
-        spec_weight[0] * dual_real[:, None] + spec_weight[1] * dual_imag[:, None], axis=2
-    )
-    back_imag = jnp.sum(
-        spec_weight[0] * dual_imag[:, None] - spec_weight[1] * dual_real[:, None], axis=2
-    )
+    field_real = field_spectrum[0]
+    field_imag = field_spectrum[1]
+    dual_real = dual_modes[0] * doubling
+    dual_imag = dual_modes[1] * doubling
+    left = jnp.stack([field_real, field_real])[:, :, :, None]
+    left_swap = jnp.stack([field_imag, -field_imag])[:, :, :, None]
+    right = jnp.stack([dual_real, dual_imag])[:, :, None]
+    right_swap = jnp.stack([dual_imag, dual_real])[:, :, None]
+    grad_weight = left * right + left_swap * right_swap
+    back_real = spec_weight[0][:, :, 0] * dual_real[:, :1] + spec_weight[1][:, :, 0] * dual_imag[:, :1]
+    back_imag = spec_weight[0][:, :, 0] * dual_imag[:, :1] - spec_weight[1][:, :, 0] * dual_real[:, :1]
+    for out_channel in range(1, channels):
+        weight_real = spec_weight[0][:, :, out_channel]
+        weight_imag = spec_weight[1][:, :, out_channel]
+        dual_r = dual_real[:, out_channel : out_channel + 1]
+        dual_i = dual_imag[:, out_channel : out_channel + 1]
+        back_real = back_real + (weight_real * dual_r + weight_imag * dual_i)
+        back_imag = back_imag + (weight_real * dual_i - weight_imag * dual_r)
     backward = jnp.stack([back_real, back_imag])
     y_parts = lax.axis_size("gy")
     y_chunks = y_table.reshape(2, 2, KY, y_parts, y_local)

time: 317 us -> 307 us (0.968)
  other arithmetic: 49.7 us -> 28.3 us
  local copies, waits for them, and re-layouts: 82 us -> 100 us
  waiting for transfers between devices: 79.1 us -> 69.8 us
    all_to_all x2, waiting for transfers between devices: 44.7 us -> 25.1 us  [field_modes(): lax.all_to_all(spectra, 'gx', split_axis=0, concat_axis=0, tiled=True)]
    another operation x1 -> x3, other arithmetic: 17.3 us -> 1.16 us  [the longest x1 1.03 us: per_device(): right = jnp.stack([dual_real, dual_imag])[:, :, None]]
    squeeze x0 -> x1, local copies, waits for them, and re-layouts: none -> 11.9 us  [per_device(): spec_weight[1][:, :, 0] * dual_imag[:, :1]]
    all_to_all x1, waiting for transfers between devices: 24.8 us -> 36.5 us  [per_device(): lax.all_to_all(x_spread, 'gx', split_axis=0, concat_axis=0, tiled=True)]
    reduce_sum x1 -> x0, other arithmetic: 9.31 us -> none  [per_device(): jnp.sum(spec_weight[0] * dual_real[:, None] + spec_weight[1] * dual_imag[...]
    unnamed x46 -> x54, local copies, waits for them, and re-layouts: 1.11 us -> 5.35 us
    add x1 -> x3, other arithmetic: 12.6 us -> 15.7 us  [the longest x1 7.37 us: per_device(): grad_weight = left * right + left_swap * right_swap]
    slice x1 -> x5, local copies, waits for them, and re-layouts: 15.8 us -> 17 us  [the longest x1 16.5 us: per_device(): spec_weight[1][:, :, 0] * dual_imag[:, :1]]
  transfers between devices with their start and end apart: 6 -> 6, of which waited for: 5 -> 4; matrix products, arithmetic and copies ran while one was open for 41% -> 40% of each run, Pallas kernels for 0% -> 0%
where the time goes in v1:
time: 307 us; the launch traced here: 301 us
  local copies, waits for them, and re-layouts  100 us (33%)
  waiting for transfers between devices  69.8 us (23%)
  matrix products  62.9 us (20%)
  starting transfers between devices  38 us (12%)
  other arithmetic  28.3 us (9%)
    all_to_all x1, waiting for transfers between devices, per_device(): lax.all_to_all(x_spread, 'gx', split_axis=0, concat_axis=0, tiled=True)  36.5 us
    another operation x10, local copies, waits for them, and re-layouts, field_modes(): jnp.stack(slabs, axis=1)  26.3 us
    all_to_all x2, waiting for transfers between devices, field_modes(): lax.all_to_all(spectra, 'gx', split_axis=0, concat_axis=0, tiled=True)  25.1 us
    slice x1, local copies, waits for them, and re-layouts, per_device(): spec_weight[1][:, :, 0] * dual_imag[:, :1]  16.5 us
    dot_general x8, matrix products, depth_forward(): lax.dot_general(depth_tail, flat_rows, tail_contract, preferred_element_t...  15.5 us
    dot_general x8, matrix products, depth_forward(): lax.dot_general(depth_lead, flat_rows, tail_contract, preferred_element_t...  15.3 us
    all_to_all x2, starting transfers between devices, field_modes(): lax.all_to_all(spectra, 'gx', split_axis=0, concat_axis=0, tiled=True)  15.2 us
    dot_general x2, matrix products, field_modes(): jnp.einsum('pqkbx,bxqjn->pkjn', x_blocks, section, precision=split_precis...  12.8 us
  transfers between devices with their start and end apart: 6, of which 4 were waited for; matrix products, arithmetic and copies ran while one was open for 40% of the time, Pallas kernels for 0%

profile of v1, /device:TPU:37, one launch (start us, length us, event | category | flops | bytes accessed | tf_op | source)
XLA Modules:
  0.0 301.2 jit_solution(9183855029259762192)
XLA Ops:
  0.7 3.3 %cosine_multiply_fusion = (f32[1,32,6,1024]{3,1,0,2:T(8,128)S(1)}, f32[1,32,6,1024]{3,1,0,2:T(8,128)S(1)}) fusion(s32[1024]{0:T(1024)S(1)} %get-tuple-element.74, s32[32,6]{0,1:T(8,128)S(1)} %get-tuple-element.73, s32[1024]{0:T(1024)S(1)} %get-tuple-element.75, s32[32,6]{0,1:T(8,128)S(1)} %get-tuple-element.72), kind=kLoop, calls=%fused_computation.50 | loop fusion | flops 4128768 | bytes 1582592 | tf_op jit(solution)/shard_map/mul | solution.py:54
  5.9 5.6 %fusion.141 = (bf16[20,1,32,1024]{3,2,1,0:T(8,128)(2,1)}, bf16[20,1,32,1024]{3,2,1,0:T(8,128)(2,1)}, bf16[20,1,32,1024]{3,2,1,0:T(8,128)(2,1)}, bf16[20,1,32,1024]{3,2,1,0:T(8,128)(2,1)}) fusion(bf16[20,4,32,1024]{3,2,1,0:T(8,128)(2,1)} %param.4), kind=kLoop, calls=%fused_computation.330 | loop fusion | bytes 10485760 | tf_op jit(solution)/shard_map/slice | solution.py:92
  31.2 2.5 stack.90
  42.1 4.5 %copy.391 = f32[32,4,2,6,640]{4,1,2,3,0:T(4,128)} copy(f32[32,4,2,6,640]{4,3,2,0,1:T(8,128)S(1)} %pad_maximum_fusion) | data formatting | bytes 7864320 | tf_op jit(solution)/shard_map/stack | solution.py:97
  46.5 9.1 %all-to-all-start = ((f32[32,4,2,6,640]{4,1,2,3,0:T(4,128)}), f32[32,4,2,6,640]{4,1,2,3,0:T(4,128)}, u32[]{:S(2)}, u32[]{:S(2)}) async-start(f32[32,4,2,6,640]{4,1,2,3,0:T(4,128)} %copy.391), calls=%async_computation | async-start | bytes 7864320 | tf_op jit(solution)/shard_map/all_to_all | solution.py:100
  55.7 4.9 %fusion.140 = (bf16[20,1,32,1024]{3,2,1,0:T(8,128)(2,1)S(1)}, bf16[20,1,32,1024]{3,2,1,0:T(8,128)(2,1)}, bf16[20,1,32,1024]{3,2,1,0:T(8,128)(2,1)S(1)}, bf16[20,1,32,1024]{3,2,1,0:T(8,128)(2,1)}) fusion(bf16[20,4,32,1024]{3,2,1,0:T(8,128)(2,1)} %param.3), kind=kLoop, calls=%fused_computation.329 | loop fusion | bytes 10485760 | tf_op jit(solution)/shard_map/slice | solution.py:92
  64.6 2.5 fusion.151
  79.2 2.9 fusion.149
  82.1 25.1 %all-to-all-done = f32[32,4,2,6,640]{4,1,2,3,0:T(4,128)} async-done(((f32[32,4,2,6,640]{4,1,2,3,0:T(4,128)}), f32[32,4,2,6,640]{4,1,2,3,0:T(4,128)}, u32[]{:S(2)}, u32[]{:S(2)}) %all-to-all-start) | async-done | bytes 3932192 | tf_op jit(solution)/shard_map/all_to_all | solution.py:100
  107.2 6.5 %fusion.13 = f32[4,2,6,6,640]{4,2,3,0,1:T(8,128)S(1)} fusion(f32[32,4,2,6,640,1,1]{4,1,2,3,0,6,5:T(4,128)} %bitcast.10, f32[2,4,6,32,2,4,1]{3,5,4,2,1,0,6:T(4,128)} %bitcast.860), kind=kOutput, calls=%fused_computation.22 | convolution fusion | flops 283115520 | bytes 4718592 | tf_op jit(solution)/shard_map/pqkbx,bxqjn->pkjn/dot_general | solution.py:101
  115.1 4.8 %all-to-all-start.1 = ((f32[4,2,6,6,640]{4,1,3,2,0:T(2,128)}), f32[4,2,6,6,640]{4,1,3,2,0:T(2,128)}, u32[]{:S(2)}, u32[]{:S(2)}) async-start(f32[4,2,6,6,640]{4,1,3,2,0:T(2,128)} %copy.394), calls=%async_computation.1 | async-start | bytes 1474560 | tf_op jit(solution)/shard_map/all_to_all | solution.py:104
  119.9 3.0 convolution_add_fusion.3
  127.5 4.5 %copy.521 = f32[32,4,2,6,640]{4,1,2,3,0:T(4,128)} copy(f32[32,4,2,6,640]{4,3,2,0,1:T(8,128)S(1)} %pad_maximum_fusion.1) | data formatting | bytes 7864320 | tf_op jit(solution)/shard_map/stack | solution.py:97
  132.0 6.1 %all-to-all-start.4 = ((f32[32,4,2,6,640]{4,1,2,3,0:T(4,128)}), f32[32,4,2,6,640]{4,1,2,3,0:T(4,128)}, u32[]{:S(2)}, u32[]{:S(2)}) async-start(f32[32,4,2,6,640]{4,1,2,3,0:T(4,128)} %copy.521), calls=%async_computation.4 | async-start | bytes 7864320 | tf_op jit(solution)/shard_map/all_to_all | solution.py:100
  138.1 16.5 %fusion.139 = (f32[1,6,20,20,6,24]{5,0,4,3,2,1:T(1,128)}, f32[1,6,20,20,6,24]{5,0,4,3,2,1:T(1,128)}) fusion(f32[2,6,20,20,6,24]{5,0,4,3,2,1:T(2,128)} %param.5), kind=kLoop, calls=%fused_computation.328 | loop fusion | bytes 5529600 | tf_op jit(solution)/shard_map/slice | solution.py:121
  155.5 11.9 %copy_bitcast_fusion = (f32[6,20,20,6,24]{4,1,3,0,2:T(8,128)}, f32[6,20,20,6,24]{4,1,3,0,2:T(8,128)}) fusion(f32[1,6,20,20,6,24]{5,0,4,3,2,1:T(1,128)} %get-tuple-element.2, f32[1,6,20,20,6,24]{5,0,4,3,2,1:T(1,128)} %get-tuple-element.3), kind=kLoop, calls=%fused_computation.2 | loop fusion | bytes 5529600 | tf_op jit(solution)/shard_map/squeeze | solution.py:121
  167.4 2.8 reshape.1573
  170.2 2.6 fusion.8
  175.0 5.6 %fusion.27 = f32[1,6,20,6,24]{4,2,0,3,1:T(8,128)S(1)} fusion(f32[6,20,20,6,24]{4,1,3,0,2:T(8,128)} %get-tuple-element.71, f32[6,20,20,6,24]{4,1,3,0,2:T(8,128)S(1)} %copy-done, f32[6,6,24]{2,1,0:T(8,128)S(1)} %bitcast.862, f32[6,6,24]{2,1,0:T(8,128)S(1)} %bitcast.864, f32[6,6,24]{2,1,0:T(8,128)S(1)} %bitcast.866, f32[6,6,24]{2,1,0:T(8,128)S(1)} %bitcast.868, ...), kind=kLoop, calls=%fused_computation.55 | loop fusion | flops 1365120 | bytes 2972160 | tf_op jit(solution)/shard_map/add | solution.py:129
  181.1 2.8 fusion.65
  189.9 6.0 %all-to-all-start.2 = ((f32[4,2,6,6,640]{4,1,3,2,0:T(2,128)}), f32[4,2,6,6,640]{4,1,3,2,0:T(2,128)S(1)}, u32[]{:S(2)}, u32[]{:S(2)}) async-start(f32[4,2,6,6,640]{4,1,3,2,0:T(2,128)} %copy.593), calls=%async_computation.2 | async-start | bytes 1474560 | tf_op jit(solution)/shard_map/all_to_all | solution.py:135
  195.9 6.4 %fusion.16 = f32[4,2,6,6,640]{4,2,3,0,1:T(8,128)S(1)} fusion(f32[32,4,2,6,640,1,1]{4,1,2,3,0,6,5:T(4,128)} %bitcast.202, f32[2,4,6,32,2,4,1]{3,5,4,2,1,0,6:T(4,128)S(1)} %bitcast.861), kind=kOutput, calls=%fused_computation.23 | convolution fusion | flops 283115520 | bytes 4718592 | tf_op jit(solution)/shard_map/pqkbx,bxqjn->pkjn/dot_general | solution.py:101
  203.7 3.8 %all-to-all-done.2 = f32[4,2,6,6,640]{4,1,3,2,0:T(2,128)S(1)} async-done(((f32[4,2,6,6,640]{4,1,3,2,0:T(2,128)}), f32[4,2,6,6,640]{4,1,3,2,0:T(2,128)S(1)}, u32[]{:S(2)}, u32[]{:S(2)}) %all-to-all-start.2) | async-done | bytes 737312 | tf_op jit(solution)/shard_map/all_to_all | solution.py:135
  207.5 4.4 %all-to-all-start.5 = ((f32[4,2,6,6,640]{4,1,3,2,0:T(2,128)}), f32[4,2,6,6,640]{4,1,3,2,0:T(2,128)S(1)}, u32[]{:S(2)}, u32[]{:S(2)}) async-start(f32[4,2,6,6,640]{4,1,3,2,0:T(2,128)} %copy.524), calls=%async_computation.5 | async-start | bytes 1474560 | tf_op jit(solution)/shard_map/all_to_all | solution.py:104
  214.3 5.0 %copy.518 = f32[32,4,2,6,640]{4,2,3,1,0:T(2,128)} copy(f32[32,4,2,6,640]{4,0,2,3,1:T(8,128)S(1)} %convolution_bitcast_fusion) | data formatting | bytes 7864320 | tf_op jit(solution)/shard_map/pqsabx,spajn->bxqjn/transpose | solution.py:137
  219.2 4.3 %all-to-all-done.5 = f32[4,2,6,6,640]{4,1,3,2,0:T(2,128)S(1)} async-done(((f32[4,2,6,6,640]{4,1,3,2,0:T(2,128)}), f32[4,2,6,6,640]{4,1,3,2,0:T(2,128)S(1)}, u32[]{:S(2)}, u32[]{:S(2)}) %all-to-all-start.5) | async-done | bytes 737312 | tf_op jit(solution)/shard_map/all_to_all | solution.py:104
  224.4 7.6 %all-to-all-start.3 = ((f32[32,4,2,6,640]{4,2,3,1,0:T(2,128)}), f32[32,4,2,6,640]{4,2,3,1,0:T(2,128)}, u32[]{:S(2)}, u32[]{:S(2)}) async-start(f32[32,4,2,6,640]{4,2,3,1,0:T(2,128)} %copy.518), calls=%async_computation.3 | async-start | bytes 7864320 | tf_op jit(solution)/shard_map/all_to_all | solution.py:138
  234.7 2.8 reshape.1587
  243.0 7.4 %multiply_add_fusion = f32[2,6,20,20,6,24]{5,0,4,3,2,1:T(2,128)} fusion(f32[2,6,20,6,24]{4,0,3,2,1:T(2,128)S(1)} %copy-done.17, f32[2,6,20,6,24]{4,0,3,2,1:T(2,128)S(1)} %copy.527, f32[2,6,20,6,24]{4,0,3,2,1:T(2,128)S(1)} %copy.526, f32[2,6,20,6,24]{4,0,3,2,1:T(2,128)S(1)} %copy.525), kind=kLoop, calls=%fused_computation | loop fusion | flops 2073600 | bytes 3317760 | tf_op jit(solution)/shard_map/add | solution.py:120
  250.4 36.5 %all-to-all-done.3 = f32[32,4,2,6,640]{4,2,3,1,0:T(2,128)} async-done(((f32[32,4,2,6,640]{4,2,3,1,0:T(2,128)}), f32[32,4,2,6,640]{4,2,3,1,0:T(2,128)}, u32[]{:S(2)}, u32[]{:S(2)}) %all-to-all-start.3) | async-done | bytes 3932192 | tf_op jit(solution)/shard_map/all_to_all | solution.py:138
  286.9 10.8 %bitcast_convert_fusion = bf16[4,640,1024]{2,1,0:T(8,128)(2,1)S(1)} fusion(f32[32,4,2,6,640]{4,2,3,1,0:T(2,128)} %all-to-all-done.3, f32[1,32,6,1024]{3,1,0,2:T(8,128)S(1)} %copy-done.6, f32[1,32,6,1024]{3,1,0,2:T(8,128)S(1)} %copy-done.4), kind=kOutput, calls=%fused_computation.1 | convolution fusion | flops 6042812416 | bytes 10747904 | tf_op jit(solution)/shard_map/sxqjn,qsjz->xnz/dot_general | solution.py:140
  297.8 3.0 copy.671
  (162 shorter events, 73.8 us)
Async XLA Ops:
  4.0 0.9 copy-start.3
  4.0 1.2 copy-start.5
  5.9 10.1 %copy-start.22 = (bf16[384,1024]{1,0:T(8,128)(2,1)}, bf16[384,1024]{1,0:T(8,128)(2,1)S(1)}, u32[]{:S(2)}) copy-start(bf16[384,1024]{1,0:T(8,128)(2,1)S(1)} %convert_element_type.114) | copy-start | bytes 2359300
  15.7 1.3 copy-start.13
  19.6 1.6 copy-start.10
  25.0 2.5 copy-start.9
  31.2 2.5 copy-start.8
  37.4 2.5 copy-start.11
  46.5 60.6 %all-to-all-start = ((f32[32,4,2,6,640]{4,1,2,3,0:T(4,128)}), f32[32,4,2,6,640]{4,1,2,3,0:T(4,128)}, u32[]{:S(2)}, u32[]{:S(2)}) async-start(f32[32,4,2,6,640]{4,1,2,3,0:T(4,128)} %copy.391), calls=%async_computation | async-start | bytes 7864320 | tf_op jit(solution)/shard_map/all_to_all | solution.py:100
  55.7 4.9 %copy-start.23 = (bf16[384,1024]{1,0:T(8,128)(2,1)S(1)}, bf16[384,1024]{1,0:T(8,128)(2,1)}, u32[]{:S(2)}) copy-start(bf16[384,1024]{1,0:T(8,128)(2,1)} %copy-done.22) | copy-start | bytes 2359300
  64.6 2.5 copy-start.14
  71.3 2.5 copy-start.12
  115.1 16.9 %all-to-all-start.1 = ((f32[4,2,6,6,640]{4,1,3,2,0:T(2,128)}), f32[4,2,6,6,640]{4,1,3,2,0:T(2,128)}, u32[]{:S(2)}, u32[]{:S(2)}) async-start(f32[4,2,6,6,640]{4,1,3,2,0:T(2,128)} %copy.394), calls=%async_computation.1 | async-start | bytes 1474560 | tf_op jit(solution)/shard_map/all_to_all | solution.py:104
  122.9 2.5 copy-start.7
  132.0 57.9 %all-to-all-start.4 = ((f32[32,4,2,6,640]{4,1,2,3,0:T(4,128)}), f32[32,4,2,6,640]{4,1,2,3,0:T(4,128)}, u32[]{:S(2)}, u32[]{:S(2)}) async-start(f32[32,4,2,6,640]{4,1,2,3,0:T(4,128)} %copy.521), calls=%async_computation.4 | async-start | bytes 7864320 | tf_op jit(solution)/shard_map/all_to_all | solution.py:100
  170.2 4.8 %copy-start = (f32[6,20,20,6,24]{4,1,3,0,2:T(8,128)S(1)}, f32[6,20,20,6,24]{4,1,3,0,2:T(8,128)}, u32[]{:S(2)}) copy-start(f32[6,20,20,6,24]{4,1,3,0,2:T(8,128)} %get-tuple-element.70) | copy-start | bytes 4147204
  172.9 0.9 copy-start.1
  174.9 5.7 %slice-start = ((s8[8847360]{0:T(1024)(128)(4,1)}), s8[4194304]{0:T(1024)(128)(4,1)S(1)}, s32[]{:S(2)}) async-start(s8[8847360]{0:T(1024)(128)(4,1)} %bitcast.836), calls=%async_computation.6 | async-start | bytes 8388608
  175.0 6.1 %slice-start.1 = ((s8[8847360]{0:T(1024)(128)(4,1)}), s8[4194304]{0:T(1024)(128)(4,1)S(1)}, s32[]{:S(2)}) async-start(s8[8847360]{0:T(1024)(128)(4,1)} %bitcast.836), calls=%async_computation.7 | async-start | bytes 8388608
  175.0 6.1 %slice-start.2 = ((s8[8847360]{0:T(1024)(128)(4,1)}), s8[458752]{0:T(1024)(128)(4,1)S(1)}, s32[]{:S(2)}) async-start(s8[8847360]{0:T(1024)(128)(4,1)} %bitcast.836), calls=%async_computation.8 | async-start | bytes 917504
  181.1 2.8 copy-start.19
  181.1 2.8 copy-start.20
  181.1 2.8 copy-start.21
  187.5 8.4 %copy-start.18 = (f32[2,2,24,32,4]{3,4,1,2,0:T(4,128)S(1)}, f32[2,2,24,32,4]{3,4,1,2,0:T(4,128)}, u32[]{:S(2)}) copy-start(f32[2,2,24,32,4]{3,4,1,2,0:T(4,128)} %maximum_maximum_fusion) | copy-start | bytes 147460
  189.9 17.6 %all-to-all-start.2 = ((f32[4,2,6,6,640]{4,1,3,2,0:T(2,128)}), f32[4,2,6,6,640]{4,1,3,2,0:T(2,128)S(1)}, u32[]{:S(2)}, u32[]{:S(2)}) async-start(f32[4,2,6,6,640]{4,1,3,2,0:T(2,128)} %copy.593), calls=%async_computation.2 | async-start | bytes 1474560 | tf_op jit(solution)/shard_map/all_to_all | solution.py:135
  207.5 16.1 %all-to-all-start.5 = ((f32[4,2,6,6,640]{4,1,3,2,0:T(2,128)}), f32[4,2,6,6,640]{4,1,3,2,0:T(2,128)S(1)}, u32[]{:S(2)}, u32[]{:S(2)}) async-start(f32[4,2,6,6,640]{4,1,3,2,0:T(2,128)} %copy.524), calls=%async_computation.5 | async-start | bytes 1474560 | tf_op jit(solution)/shard_map/all_to_all | solution.py:104
  219.2 12.8 %copy-start.2 = (f32[6,6,20,2,24,1,1]{4,2,1,0,3,5,6:T(8,128)S(1)}, f32[6,6,20,2,24,1,1]{4,2,1,0,3,5,6:T(8,128)}, u32[]{:S(2)}) copy-start(f32[6,6,20,2,24,1,1]{4,2,1,0,3,5,6:T(8,128)} %copy-done.1) | copy-start | bytes 414724
  224.4 62.5 %all-to-all-start.3 = ((f32[32,4,2,6,640]{4,2,3,1,0:T(2,128)}), f32[32,4,2,6,640]{4,2,3,1,0:T(2,128)}, u32[]{:S(2)}, u32[]{:S(2)}) async-start(f32[32,4,2,6,640]{4,2,3,1,0:T(2,128)} %copy.518), calls=%async_computation.3 | async-start | bytes 7864320 | tf_op jit(solution)/shard_map/all_to_all | solution.py:138
  240.1 1.2 copy-start.15
  241.9 1.1 copy-start.17
  243.0 43.9 %copy-start.4 = (f32[1,32,6,1024]{3,1,0,2:T(8,128)S(1)}, f32[1,32,6,1024]{3,1,0,2:T(8,128)}, u32[]{:S(2)}) copy-start(f32[1,32,6,1024]{3,1,0,2:T(8,128)} %copy-done.3) | copy-start | bytes 2359300
  243.0 43.9 %copy-start.6 = (f32[1,32,6,1024]{3,1,0,2:T(8,128)S(1)}, f32[1,32,6,1024]{3,1,0,2:T(8,128)}, u32[]{:S(2)}) copy-start(f32[1,32,6,1024]{3,1,0,2:T(8,128)} %copy-done.5) | copy-start | bytes 2359300
  (1 other events, 0.9 us)

commit v2 on v1

--- a/solution.py
+++ b/solution.py
@@ -79,26 +79,20 @@
     kx_local = KX // y_parts
     y_split = y_table.reshape(2, 2, KY, y_parts, y_local)
 
-    def depth_forward(flat_rows):
-        first = lax.dot_general(
-            depth_lead, flat_rows, tail_contract, preferred_element_type=jnp.float32
-        )
+    def depth_forward(planes):
+        contract = (((1,), (2,)), ((), ()))
+        first = lax.dot_general(depth_lead, planes, contract, preferred_element_type=jnp.float32)
         return first + lax.dot_general(
-            depth_tail, flat_rows, tail_contract, preferred_element_type=jnp.float32
+            depth_tail, planes, contract, preferred_element_type=jnp.float32
         )
 
     def field_modes(field):
-        slabs = [
-            depth_forward(field[:, plane].reshape(channels * y_local, depth_time)).reshape(
-                x_groups, 2 * mode_local, channels * y_local
-            )
-            for plane in range(x_local)
-        ]
-        spectra = jnp.stack(slabs, axis=1).reshape(
-            x_groups, x_local, 2, mode_local, channels * y_local
+        planes = field.transpose(1, 0, 2, 3).reshape(x_local, channels * y_local, depth_time)
+        spectra = depth_forward(planes).reshape(
+            x_groups, 2, mode_local, x_local, channels * y_local
         )
         section = lax.all_to_all(spectra, "gx", split_axis=0, concat_axis=0, tiled=True)
-        summed_x = jnp.einsum("pqkbx,bxqjn->pkjn", x_blocks, section, precision=split_precision)
+        summed_x = jnp.einsum("pqkbx,bqjxn->pkjn", x_blocks, section, precision=split_precision)
         summed_x = summed_x.reshape(2, y_parts, kx_local, mode_local, channels * y_local)
         summed_x = summed_x.transpose(1, 0, 2, 3, 4)
         gathered = lax.all_to_all(summed_x, "gy", split_axis=0, concat_axis=0, tiled=True)

time: 307 us -> 290 us (0.945)
  waiting for transfers between devices: 69.8 us -> 90.7 us
  local copies, waits for them, and re-layouts: 100 us -> 81.7 us
  matrix products: 62.9 us -> 49.4 us
  starting transfers between devices: 38 us -> 34.7 us
    another operation x10 -> x0, local copies, waits for them, and re-layouts: 26.3 us -> none  [field_modes(): jnp.stack(slabs, axis=1)]
    all_to_all x2, waiting for transfers between devices: 25.1 us -> 45 us  [field_modes(): lax.all_to_all(spectra, 'gx', split_axis=0, concat_axis=0, tiled=True)]
    dot_general x18 -> x6, matrix products: 43.7 us -> 30.1 us  [the longest x2 12.9 us: field_modes(): jnp.einsum('pqkbx,bqjxn->pkjn', x_blocks, section, precision=split_precis...]
    slice x2 -> x0, local copies, waits for them, and re-layouts: 10.5 us -> none  [field_modes(): field[:, plane].reshape(channels * y_local, depth_time)]
    unnamed x54 -> x52, local copies, waits for them, and re-layouts: 5.35 us -> 15.3 us
    reshape x0 -> x2, local copies, waits for them, and re-layouts: none -> 5.19 us  [field_modes(): depth_forward(planes)]
    add x0 -> x2, local copies, waits for them, and re-layouts: none -> 5.06 us  [depth_forward(): first + lax.dot_general(depth_tail, planes, contract, preferred_element_t...]
    another operation x2 -> x0, other arithmetic: 4.38 us -> none  [field_modes(): jnp.stack(slabs, axis=1)]
  transfers between devices with their start and end apart: 6 -> 6, of which waited for: 4 -> 6; matrix products, arithmetic and copies ran while one was open for 40% -> 36% of each run, Pallas kernels for 0% -> 0%
where the time goes in v2:
time: 290 us; the launch traced here: 284 us
  waiting for transfers between devices  90.7 us (31%)
  local copies, waits for them, and re-layouts  81.7 us (28%)
  matrix products  49.4 us (17%)
  starting transfers between devices  34.7 us (12%)
  other arithmetic  25.7 us (9%)
    all_to_all x2, waiting for transfers between devices, field_modes(): lax.all_to_all(spectra, 'gx', split_axis=0, concat_axis=0, tiled=True)  45 us
    all_to_all x1, waiting for transfers between devices, per_device(): lax.all_to_all(x_spread, 'gx', split_axis=0, concat_axis=0, tiled=True)  37 us
    slice x1, local copies, waits for them, and re-layouts, per_device(): spec_weight[1][:, :, 0] * dual_imag[:, :1]  16.4 us
    unnamed x52, local copies, waits for them, and re-layouts  15.3 us
    all_to_all x2, starting transfers between devices, field_modes(): lax.all_to_all(spectra, 'gx', split_axis=0, concat_axis=0, tiled=True)  14.6 us
    dot_general x2, matrix products, field_modes(): jnp.einsum('pqkbx,bqjxn->pkjn', x_blocks, section, precision=split_precis...  12.9 us
    squeeze x1, local copies, waits for them, and re-layouts, per_device(): spec_weight[1][:, :, 0] * dual_imag[:, :1]  11.9 us
    dot_general x1, matrix products, per_device(): jnp.einsum('sxqjn,qsjz->xnz', section, depth_parts, precision=split_preci...  10.8 us
  transfers between devices with their start and end apart: 6, of which 6 were waited for; matrix products, arithmetic and copies ran while one was open for 36% of the time, Pallas kernels for 0%

profile of v2, /device:TPU:37, one launch (start us, length us, event | category | flops | bytes accessed | tf_op | source)
XLA Modules:
  0.0 284.1 jit_solution(7185061034741684128)
XLA Ops:
  0.7 3.3 %cosine_multiply_fusion = (f32[1,32,6,1024]{3,1,0,2:T(8,128)S(1)}, f32[1,32,6,1024]{3,1,0,2:T(8,128)S(1)}) fusion(s32[1024]{0:T(1024)S(1)} %get-tuple-element.66, s32[32,6]{0,1:T(8,128)S(1)} %get-tuple-element.65, s32[1024]{0:T(1024)S(1)} %get-tuple-element.67, s32[32,6]{0,1:T(8,128)S(1)} %get-tuple-element.64), kind=kLoop, calls=%fused_computation.43 | loop fusion | flops 4128768 | bytes 1582592 | tf_op jit(solution)/shard_map/mul | solution.py:54
  6.9 6.0 %copy.387 = bf16[20,4,32,1024]{3,2,0,1:T(8,128)(2,1)} copy(bf16[20,4,32,1024]{3,2,1,0:T(8,128)(2,1)} %param.4) | data formatting | bytes 10485760 | tf_op args[1]
  16.9 4.9 %fusion.146 = f32[384,4,640]{2,0,1:T(8,128)S(1)} fusion(bf16[384,1024,1]{1,0,2:T(8,128)(2,1)S(1)} %reshape.1562, bf16[4,640,1024]{2,1,0:T(8,128)(2,1)} %bitcast.822), kind=kOutput, calls=%fused_computation.325 | convolution fusion | flops 2013265920 | bytes 9961472 | tf_op jit(solution)/shard_map/dot_general | solution.py:84
  26.7 2.6 copy.390
  29.3 8.9 %all-to-all-start = ((f32[32,2,6,4,640]{4,3,1,2,0:T(4,128)}), f32[32,2,6,4,640]{4,3,1,2,0:T(4,128)}, u32[]{:S(2)}, u32[]{:S(2)}) async-start(f32[32,2,6,4,640]{4,3,1,2,0:T(4,128)} %copy.390), calls=%async_computation | async-start | bytes 7864320 | tf_op jit(solution)/shard_map/all_to_all | solution.py:94
  38.2 3.1 %copy.520 = bf16[20,4,32,1024]{3,2,0,1:T(8,128)(2,1)S(1)} copy(bf16[20,4,32,1024]{3,2,1,0:T(8,128)(2,1)} %param.3) | data formatting | bytes 10485760 | tf_op args[0]
  43.7 4.2 %fusion.147 = f32[384,4,640]{2,0,1:T(8,128)} fusion(bf16[384,1024,1]{1,0,2:T(8,128)(2,1)S(1)} %reshape.1562, bf16[4,640,1024]{2,1,0:T(8,128)(2,1)S(1)} %bitcast.820), kind=kOutput, calls=%fused_computation.326 | convolution fusion | flops 2013265920 | bytes 9961472 | tf_op jit(solution)/shard_map/dot_general | solution.py:84
  47.8 42.0 %all-to-all-done = f32[32,2,6,4,640]{4,3,1,2,0:T(4,128)} async-done(((f32[32,2,6,4,640]{4,3,1,2,0:T(4,128)}), f32[32,2,6,4,640]{4,3,1,2,0:T(4,128)}, u32[]{:S(2)}, u32[]{:S(2)}) %all-to-all-start) | async-done | bytes 3932192 | tf_op jit(solution)/shard_map/all_to_all | solution.py:94
  89.9 6.4 %fusion.13 = f32[4,2,6,6,640]{4,2,3,0,1:T(8,128)S(1)} fusion(f32[32,2,6,4,640,1,1]{4,3,1,2,0,6,5:T(4,128)} %bitcast.11, f32[2,4,6,32,2,4,1]{3,5,4,2,1,0,6:T(4,128)S(1)} %bitcast.830), kind=kOutput, calls=%fused_computation.22 | convolution fusion | flops 283115520 | bytes 4718592 | tf_op jit(solution)/shard_map/pqkbx,bqjxn->pkjn/dot_general | solution.py:95
  97.7 5.5 %all-to-all-start.1 = ((f32[4,2,6,6,640]{4,1,3,2,0:T(2,128)}), f32[4,2,6,6,640]{4,1,3,2,0:T(2,128)S(1)}, u32[]{:S(2)}, u32[]{:S(2)}) async-start(f32[4,2,6,6,640]{4,1,3,2,0:T(2,128)} %copy.393), calls=%async_computation.1 | async-start | bytes 1474560 | tf_op jit(solution)/shard_map/all_to_all | solution.py:98
  103.2 5.9 %convolution_add_fusion = f32[384,4,640]{2,0,1:T(8,128)S(1)} fusion(f32[384,4,640]{2,0,1:T(8,128)} %fusion.147, bf16[4,640,1024]{2,1,0:T(8,128)(2,1)} %bitcast.821, f32[384,1024]{1,0:T(8,128)S(1)} %copy-done.7, bf16[384,1024]{1,0:T(8,128)(2,1)S(1)} %copy-done.19), kind=kOutput, calls=%fused_computation.17 | convolution fusion | flops 2015428608 | bytes 15466496 | tf_op jit(solution)/shard_map/dot_general | solution.py:85
  111.7 2.6 copy.522
  115.7 5.7 %all-to-all-start.4 = ((f32[32,2,6,4,640]{4,3,1,2,0:T(4,128)}), f32[32,2,6,4,640]{4,3,1,2,0:T(4,128)}, u32[]{:S(2)}, u32[]{:S(2)}) async-start(f32[32,2,6,4,640]{4,3,1,2,0:T(4,128)} %copy.522), calls=%async_computation.4 | async-start | bytes 7864320 | tf_op jit(solution)/shard_map/all_to_all | solution.py:94
  121.4 16.4 %fusion.142 = (f32[1,6,20,20,6,24]{5,0,4,3,2,1:T(1,128)}, f32[1,6,20,20,6,24]{5,0,4,3,2,1:T(1,128)}) fusion(f32[2,6,20,20,6,24]{5,0,4,3,2,1:T(2,128)} %param.5), kind=kLoop, calls=%fused_computation.321 | loop fusion | bytes 5529600 | tf_op jit(solution)/shard_map/slice | solution.py:115
  138.8 11.9 %copy_bitcast_fusion = (f32[6,20,20,6,24]{4,1,3,0,2:T(8,128)}, f32[6,20,20,6,24]{4,1,3,0,2:T(8,128)}) fusion(f32[1,6,20,20,6,24]{5,0,4,3,2,1:T(1,128)} %get-tuple-element.2, f32[1,6,20,20,6,24]{5,0,4,3,2,1:T(1,128)} %get-tuple-element.3), kind=kLoop, calls=%fused_computation.2 | loop fusion | bytes 5529600 | tf_op jit(solution)/shard_map/squeeze | solution.py:115
  150.6 2.8 %reshape.1567 = f32[4,2,6,6,20,32,1]{5,4,1,3,2,0,6:T(8,128)S(1)} reshape(f32[4,2,6,6,640]{4,1,3,2,0:T(2,128)} %copy-done.11) | data formatting | bytes 1474560 | tf_op jit(solution)/shard_map/reshape | solution.py:99
  153.5 2.6 fusion.8
  158.3 5.6 %fusion.28 = f32[1,6,20,6,24]{4,2,0,3,1:T(8,128)S(1)} fusion(f32[6,20,20,6,24]{4,1,3,0,2:T(8,128)} %get-tuple-element.63, f32[6,20,20,6,24]{4,1,3,0,2:T(8,128)S(1)} %copy-done, f32[6,6,24]{2,1,0:T(8,128)S(1)} %bitcast.832, f32[6,6,24]{2,1,0:T(8,128)S(1)} %bitcast.834, f32[6,6,24]{2,1,0:T(8,128)S(1)} %bitcast.836, f32[6,6,24]{2,1,0:T(8,128)S(1)} %bitcast.838, ...), kind=kLoop, calls=%fused_computation.48 | loop fusion | flops 1365120 | bytes 2972160 | tf_op jit(solution)/shard_map/add | solution.py:123
  164.4 2.8 fusion.66
  173.2 3.0 %all-to-all-done.4 = f32[32,2,6,4,640]{4,3,1,2,0:T(4,128)} async-done(((f32[32,2,6,4,640]{4,3,1,2,0:T(4,128)}), f32[32,2,6,4,640]{4,3,1,2,0:T(4,128)}, u32[]{:S(2)}, u32[]{:S(2)}) %all-to-all-start.4) | async-done | bytes 3932192 | tf_op jit(solution)/shard_map/all_to_all | solution.py:94
  176.2 4.1 %all-to-all-start.2 = ((f32[4,2,6,6,640]{4,1,3,2,0:T(2,128)}), f32[4,2,6,6,640]{4,1,3,2,0:T(2,128)S(1)}, u32[]{:S(2)}, u32[]{:S(2)}) async-start(f32[4,2,6,6,640]{4,1,3,2,0:T(2,128)} %copy.594), calls=%async_computation.2 | async-start | bytes 1474560 | tf_op jit(solution)/shard_map/all_to_all | solution.py:129
  180.3 6.5 %fusion.16 = f32[4,2,6,6,640]{4,2,3,0,1:T(8,128)S(1)} fusion(f32[32,2,6,4,640,1,1]{4,3,1,2,0,6,5:T(4,128)} %bitcast.203, f32[2,4,6,32,2,4,1]{3,5,4,2,1,0,6:T(4,128)} %bitcast.831), kind=kOutput, calls=%fused_computation.23 | convolution fusion | flops 283115520 | bytes 4718592 | tf_op jit(solution)/shard_map/pqkbx,bqjxn->pkjn/dot_general | solution.py:95
  188.2 3.7 %all-to-all-done.2 = f32[4,2,6,6,640]{4,1,3,2,0:T(2,128)S(1)} async-done(((f32[4,2,6,6,640]{4,1,3,2,0:T(2,128)}), f32[4,2,6,6,640]{4,1,3,2,0:T(2,128)S(1)}, u32[]{:S(2)}, u32[]{:S(2)}) %all-to-all-start.2) | async-done | bytes 737312 | tf_op jit(solution)/shard_map/all_to_all | solution.py:129
  191.9 4.4 %all-to-all-start.5 = ((f32[4,2,6,6,640]{4,1,3,2,0:T(2,128)}), f32[4,2,6,6,640]{4,1,3,2,0:T(2,128)S(1)}, u32[]{:S(2)}, u32[]{:S(2)}) async-start(f32[4,2,6,6,640]{4,1,3,2,0:T(2,128)} %copy.525), calls=%async_computation.5 | async-start | bytes 1474560 | tf_op jit(solution)/shard_map/all_to_all | solution.py:98
  198.7 5.0 %copy.517 = f32[32,4,2,6,640]{4,2,3,1,0:T(2,128)} copy(f32[32,4,2,6,640]{4,0,2,3,1:T(8,128)S(1)} %convolution_bitcast_fusion) | data formatting | bytes 7864320 | tf_op jit(solution)/shard_map/pqsabx,spajn->bxqjn/transpose | solution.py:131
  203.6 4.3 %all-to-all-done.5 = f32[4,2,6,6,640]{4,1,3,2,0:T(2,128)S(1)} async-done(((f32[4,2,6,6,640]{4,1,3,2,0:T(2,128)}), f32[4,2,6,6,640]{4,1,3,2,0:T(2,128)S(1)}, u32[]{:S(2)}, u32[]{:S(2)}) %all-to-all-start.5) | async-done | bytes 737312 | tf_op jit(solution)/shard_map/all_to_all | solution.py:98
  208.9 6.1 %all-to-all-start.3 = ((f32[32,4,2,6,640]{4,2,3,1,0:T(2,128)}), f32[32,4,2,6,640]{4,2,3,1,0:T(2,128)}, u32[]{:S(2)}, u32[]{:S(2)}) async-start(f32[32,4,2,6,640]{4,2,3,1,0:T(2,128)} %copy.517), calls=%async_computation.3 | async-start | bytes 7864320 | tf_op jit(solution)/shard_map/all_to_all | solution.py:132
  217.6 2.8 %reshape.1581 = f32[4,2,6,6,20,32,1]{5,4,1,3,2,0,6:T(8,128)S(1)} reshape(f32[4,2,6,6,640]{4,1,3,2,0:T(2,128)} %copy-done.12) | data formatting | bytes 1474560 | tf_op jit(solution)/shard_map/reshape | solution.py:99
  225.3 7.5 %multiply_add_fusion = f32[2,6,20,20,6,24]{5,0,4,3,2,1:T(2,128)} fusion(f32[2,6,20,6,24]{4,0,3,2,1:T(2,128)S(1)} %copy-done.13, f32[2,6,20,6,24]{4,0,3,2,1:T(2,128)S(1)} %copy.528, f32[2,6,20,6,24]{4,0,3,2,1:T(2,128)S(1)} %copy.527, f32[2,6,20,6,24]{4,0,3,2,1:T(2,128)S(1)} %copy.526), kind=kLoop, calls=%fused_computation | loop fusion | flops 2073600 | bytes 3317760 | tf_op jit(solution)/shard_map/add | solution.py:114
  232.8 37.0 %all-to-all-done.3 = f32[32,4,2,6,640]{4,2,3,1,0:T(2,128)} async-done(((f32[32,4,2,6,640]{4,2,3,1,0:T(2,128)}), f32[32,4,2,6,640]{4,2,3,1,0:T(2,128)}, u32[]{:S(2)}, u32[]{:S(2)}) %all-to-all-start.3) | async-done | bytes 3932192 | tf_op jit(solution)/shard_map/all_to_all | solution.py:132
  269.9 10.8 %bitcast_convert_fusion = bf16[4,640,1024]{2,1,0:T(8,128)(2,1)S(1)} fusion(f32[32,4,2,6,640]{4,2,3,1,0:T(2,128)} %all-to-all-done.3, f32[1,32,6,1024]{3,1,0,2:T(8,128)S(1)} %copy-done.6, f32[1,32,6,1024]{3,1,0,2:T(8,128)S(1)} %copy-done.4), kind=kOutput, calls=%fused_computation.1 | convolution fusion | flops 6042812416 | bytes 10747904 | tf_op jit(solution)/shard_map/sxqjn,qsjz->xnz/dot_general | solution.py:134
  280.7 3.0 %copy.672 = bf16[4,20,32,1024]{3,2,0,1:T(8,128)(2,1)} copy(bf16[4,20,32,1024]{3,2,1,0:T(8,128)(2,1)S(1)} %bitcast.827) | data formatting | bytes 10485760 | tf_op jit(solution)/shard_map/reshape | solution.py:136
  (138 shorter events, 40.6 us)
Async XLA Ops:
  4.0 0.9 copy-start.3
  4.0 2.2 copy-start.5
  6.8 6.0 %copy-start.8 = (f32[32,2,6,1024]{3,0,1,2:T(8,128)S(1)}, f32[32,2,6,1024]{3,0,1,2:T(8,128)}, u32[]{:S(2)}) copy-start(f32[32,2,6,1024]{3,0,1,2:T(8,128)} %fusion.19) | copy-start | bytes 4718596
  15.2 6.6 %slice-start.3 = ((s8[5242880]{0:T(1024)(128)(4,1)}), s8[4194304]{0:T(1024)(128)(4,1)S(1)}, s32[]{:S(2)}) async-start(s8[5242880]{0:T(1024)(128)(4,1)} %bitcast.823), calls=%async_computation.9 | async-start | bytes 8388608
  16.9 4.9 %copy-start.18 = (bf16[384,1024]{1,0:T(8,128)(2,1)}, bf16[384,1024]{1,0:T(8,128)(2,1)S(1)}, u32[]{:S(2)}) copy-start(bf16[384,1024]{1,0:T(8,128)(2,1)S(1)} %convert_element_type.109) | copy-start | bytes 2359300
  16.9 4.9 %copy-start.7 = (f32[384,1024]{1,0:T(8,128)S(1)}, f32[384,1024]{1,0:T(8,128)}, u32[]{:S(2)}) copy-start(f32[384,1024]{1,0:T(8,128)} %reshape.1554) | copy-start | bytes 4718596
  16.9 4.9 %slice-start.4 = ((s8[5242880]{0:T(1024)(128)(4,1)}), s8[1048576]{0:T(1024)(128)(4,1)S(1)}, s32[]{:S(2)}) async-start(s8[5242880]{0:T(1024)(128)(4,1)} %bitcast.823), calls=%async_computation.10 | async-start | bytes 2097152
  29.3 60.6 %all-to-all-start = ((f32[32,2,6,4,640]{4,3,1,2,0:T(4,128)}), f32[32,2,6,4,640]{4,3,1,2,0:T(4,128)}, u32[]{:S(2)}, u32[]{:S(2)}) async-start(f32[32,2,6,4,640]{4,3,1,2,0:T(4,128)} %copy.390), calls=%async_computation | async-start | bytes 7864320 | tf_op jit(solution)/shard_map/all_to_all | solution.py:94
  41.3 2.4 copy-start.9
  41.9 47.9 %copy-start.14 = (f32[2,2,24,32,4]{3,4,1,2,0:T(4,128)}, f32[2,2,24,32,4]{3,4,1,2,0:T(4,128)S(1)}, u32[]{:S(2)}) copy-start(f32[2,2,24,32,4]{3,4,1,2,0:T(4,128)S(1)} %maximum_maximum_fusion) | copy-start | bytes 147460
  89.9 13.3 %copy-start.19 = (bf16[384,1024]{1,0:T(8,128)(2,1)S(1)}, bf16[384,1024]{1,0:T(8,128)(2,1)}, u32[]{:S(2)}) copy-start(bf16[384,1024]{1,0:T(8,128)(2,1)} %copy-done.18) | copy-start | bytes 2359300
  97.7 17.1 %all-to-all-start.1 = ((f32[4,2,6,6,640]{4,1,3,2,0:T(2,128)}), f32[4,2,6,6,640]{4,1,3,2,0:T(2,128)S(1)}, u32[]{:S(2)}, u32[]{:S(2)}) async-start(f32[4,2,6,6,640]{4,1,3,2,0:T(2,128)} %copy.393), calls=%async_computation.1 | async-start | bytes 1474560 | tf_op jit(solution)/shard_map/all_to_all | solution.py:98
  114.8 0.9 copy-start.11
  115.7 60.5 %all-to-all-start.4 = ((f32[32,2,6,4,640]{4,3,1,2,0:T(4,128)}), f32[32,2,6,4,640]{4,3,1,2,0:T(4,128)}, u32[]{:S(2)}, u32[]{:S(2)}) async-start(f32[32,2,6,4,640]{4,3,1,2,0:T(4,128)} %copy.522), calls=%async_computation.4 | async-start | bytes 7864320 | tf_op jit(solution)/shard_map/all_to_all | solution.py:94
  153.5 4.8 %copy-start = (f32[6,20,20,6,24]{4,1,3,0,2:T(8,128)S(1)}, f32[6,20,20,6,24]{4,1,3,0,2:T(8,128)}, u32[]{:S(2)}) copy-start(f32[6,20,20,6,24]{4,1,3,0,2:T(8,128)} %get-tuple-element.62) | copy-start | bytes 4147204
  156.2 0.9 copy-start.1
  158.2 5.7 %slice-start = ((s8[8847360]{0:T(1024)(128)(4,1)}), s8[4194304]{0:T(1024)(128)(4,1)S(1)}, s32[]{:S(2)}) async-start(s8[8847360]{0:T(1024)(128)(4,1)} %bitcast.814), calls=%async_computation.6 | async-start | bytes 8388608
  158.3 6.1 %slice-start.1 = ((s8[8847360]{0:T(1024)(128)(4,1)}), s8[4194304]{0:T(1024)(128)(4,1)S(1)}, s32[]{:S(2)}) async-start(s8[8847360]{0:T(1024)(128)(4,1)} %bitcast.814), calls=%async_computation.7 | async-start | bytes 8388608
  158.3 6.1 %slice-start.2 = ((s8[8847360]{0:T(1024)(128)(4,1)}), s8[458752]{0:T(1024)(128)(4,1)S(1)}, s32[]{:S(2)}) async-start(s8[8847360]{0:T(1024)(128)(4,1)} %bitcast.814), calls=%async_computation.8 | async-start | bytes 917504
  164.4 2.8 copy-start.15
  164.4 2.8 copy-start.16
  164.4 2.8 copy-start.17
  176.2 15.7 %all-to-all-start.2 = ((f32[4,2,6,6,640]{4,1,3,2,0:T(2,128)}), f32[4,2,6,6,640]{4,1,3,2,0:T(2,128)S(1)}, u32[]{:S(2)}, u32[]{:S(2)}) async-start(f32[4,2,6,6,640]{4,1,3,2,0:T(2,128)} %copy.594), calls=%async_computation.2 | async-start | bytes 1474560 | tf_op jit(solution)/shard_map/all_to_all | solution.py:129
  191.9 16.1 %all-to-all-start.5 = ((f32[4,2,6,6,640]{4,1,3,2,0:T(2,128)}), f32[4,2,6,6,640]{4,1,3,2,0:T(2,128)S(1)}, u32[]{:S(2)}, u32[]{:S(2)}) async-start(f32[4,2,6,6,640]{4,1,3,2,0:T(2,128)} %copy.525), calls=%async_computation.5 | async-start | bytes 1474560 | tf_op jit(solution)/shard_map/all_to_all | solution.py:98
  203.6 11.4 %copy-start.2 = (f32[6,6,20,2,24,1,1]{4,2,1,0,3,5,6:T(8,128)S(1)}, f32[6,6,20,2,24,1,1]{4,2,1,0,3,5,6:T(8,128)}, u32[]{:S(2)}) copy-start(f32[6,6,20,2,24,1,1]{4,2,1,0,3,5,6:T(8,128)} %copy-done.1) | copy-start | bytes 414724
  208.0 0.9 copy-start.12
  208.9 61.0 %all-to-all-start.3 = ((f32[32,4,2,6,640]{4,2,3,1,0:T(2,128)}), f32[32,4,2,6,640]{4,2,3,1,0:T(2,128)}, u32[]{:S(2)}, u32[]{:S(2)}) async-start(f32[32,4,2,6,640]{4,2,3,1,0:T(2,128)} %copy.517), calls=%async_computation.3 | async-start | bytes 7864320 | tf_op jit(solution)/shard_map/all_to_all | solution.py:132
  222.9 1.2 copy-start.10
  223.1 2.2 copy-start.13
  225.3 44.5 %copy-start.4 = (f32[1,32,6,1024]{3,1,0,2:T(8,128)S(1)}, f32[1,32,6,1024]{3,1,0,2:T(8,128)}, u32[]{:S(2)}) copy-start(f32[1,32,6,1024]{3,1,0,2:T(8,128)} %copy-done.3) | copy-start | bytes 2359300
  225.3 44.5 %copy-start.6 = (f32[1,32,6,1024]{3,1,0,2:T(8,128)S(1)}, f32[1,32,6,1024]{3,1,0,2:T(8,128)}, u32[]{:S(2)}) copy-start(f32[1,32,6,1024]{3,1,0,2:T(8,128)} %copy-done.5) | copy-start | bytes 2359300
